TPU v7x, 32 devices: a whole 2x2x4 slice. The times are simulated.
32 devices in a mesh: row: 8 (over y, x, core), col: 4 (over z).
Axes of the slice: x: 2, y: 2, z: 4, core: 2. Of those that a mesh axis runs over, the one named last changes fastest.
Arguments:
- pair_rep: bfloat16 [128, 128, 128], P(('row', 'col')), may hold values from -16 to 16
- tile_mask: int32 [1, 1], replicated, may hold values from 0 to 1, as said below
- chain_ids: int32 [128], replicated, may hold values from 0 to 3, never falling along the last dimension, each value on 1 to 64 neighbouring positions
- chain_bias: float32 [2, 4], replicated, may hold values from -6 to 6
- row_project: bfloat16 [128, 512], replicated, may hold values from -0.5 to 0.5
- row_bias_proj: bfloat16 [128, 4], replicated, may hold values from -36 to 36
- row_output: bfloat16 [128, 128], replicated, may hold values from -0.5 to 0.5
- col_project: bfloat16 [128, 512], replicated, may hold values from -0.5 to 0.5
- col_bias_proj: bfloat16 [128, 4], replicated, may hold values from -36 to 36
- col_output: bfloat16 [128, 128], replicated, may hold values from -0.5 to 0.5
- tri_left: bfloat16 [128, 256], replicated, may hold values from -0.5 to 0.5
- tri_right: bfloat16 [128, 256], replicated, may hold values from -0.5 to 0.5
- tri_gate: bfloat16 [128, 128], replicated, may hold values from -0.5 to 0.5
- tri_output: bfloat16 [128, 128], replicated, may hold values from -1.5 to 1.5
Outputs:
- pair_out: bfloat16 [128, 128, 128], P('row', 'col')
Inputs may be any that keep to these rules, and one draw needn't show every extreme that they name: `tile_mask`: every diagonal entry is 1. `chain_ids`: chain numbers never fall along the residues.
All inputs are finite; a program needn't handle non-finite values.
Results may differ from a plain program's by a relative error of at most 0.018.
Values may be sent and summed in bfloat16 or wider, within the bound.
No kernel may reach another device: no remote copies, remote signals or barrier semaphores. Data moves between devices by JAX's collectives and lax.ppermute only.
A program may use at most 64 MiB of HBM per device.

v0:
```python
import jax
import jax.numpy as jnp
from jax import lax
from jax.sharding import PartitionSpec as P


def layer_norm(values):
    values = values.astype(jnp.float32)
    center = values - jnp.mean(values, axis=-1, keepdims=True)
    spread = jnp.mean(center * center, axis=-1, keepdims=True)
    return center * lax.rsqrt(spread + 1e-05)


def tile_rows(positions, tile_table, length):
    tile_count = tile_table.shape[0]
    tile_width = length // tile_count
    onehot = (positions[:, None] // tile_width == jnp.arange(tile_count)[None, :]).astype(
        jnp.float32
    )
    picked = jnp.dot(onehot, tile_table.astype(jnp.float32))
    spread_out = jnp.broadcast_to(picked[:, :, None], (positions.shape[0], tile_count, tile_width))
    return spread_out.reshape(positions.shape[0], length) > 0.5


def tile_pairs(row_pos, col_pos, tile_table, length):
    tile_count = tile_table.shape[0]
    tile_width = length // tile_count
    row_hot = (row_pos[:, None] // tile_width == jnp.arange(tile_count)[None, :]).astype(
        jnp.float32
    )
    col_hot = (col_pos[:, None] // tile_width == jnp.arange(tile_count)[None, :]).astype(
        jnp.float32
    )
    return jnp.dot(jnp.dot(row_hot, tile_table.astype(jnp.float32)), col_hot.T)


def attend_lines(
    queries,
    key_rows,
    value_rows,
    gate_pre,
    bias_all,
    key_ok,
    chain_ids,
    chain_add,
    line_dim,
    flipped,
):
    line_count = queries.shape[line_dim]
    length = queries.shape[1 - line_dim]
    head_count = queries.shape[2]
    head_size = queries.shape[3]
    width_all = head_count * head_size
    query_rows = min(128, length)
    per_line = length // query_rows
    scaling = head_size ** (-0.5)

    def one_block(block_index):
        line_index = block_index // per_line
        offset = block_index % per_line * query_rows
        query_line = lax.dynamic_index_in_dim(queries, line_index, line_dim, keepdims=False)
        query_block = lax.dynamic_slice_in_dim(query_line, offset, query_rows, 0)
        key_line = lax.dynamic_index_in_dim(key_rows, line_index, line_dim, keepdims=False)
        value_line = lax.dynamic_index_in_dim(value_rows, line_index, line_dim, keepdims=False)
        scores = (
            jnp.einsum("qhd,khd->hqk", query_block, key_line, preferred_element_type=jnp.float32)
            * scaling
        )
        if flipped:
            bias_block = lax.dynamic_slice_in_dim(bias_all, offset, query_rows, 2).transpose(
                0, 2, 1
            )
        else:
            bias_block = lax.dynamic_slice_in_dim(bias_all, offset, query_rows, 1)
        scores = scores + bias_block
        chain_block = lax.dynamic_slice_in_dim(chain_ids, offset, query_rows, 0)
        same_chain = (chain_block[:, None] == chain_ids[None, :]).astype(jnp.float32)
        scores = scores + chain_add[:, None, None] * same_chain[None]
        usable = lax.dynamic_index_in_dim(key_ok, line_index, 0, keepdims=False)
        scores = jnp.where(usable[None, None, :], scores, -1000000000.0)
        row_peak = jnp.max(scores, axis=-1, keepdims=True)
        weights = jnp.exp(scores - row_peak)
        attention = (weights / jnp.sum(weights, axis=-1, keepdims=True)).astype(jnp.bfloat16)
        mixed_rows = jnp.einsum(
            "hqk,khd->qhd", attention, value_line, preferred_element_type=jnp.float32
        ).reshape(query_rows, width_all)
        gate_line = lax.dynamic_index_in_dim(gate_pre, line_index, line_dim, keepdims=False)
        gate_block = lax.dynamic_slice_in_dim(gate_line, offset, query_rows, 0)
        return (mixed_rows * jax.nn.sigmoid(gate_block)).astype(jnp.bfloat16)

    outputs = lax.map(one_block, jnp.arange(line_count * per_line, dtype=jnp.int32))
    outputs = outputs.reshape(line_count, length, width_all)
    if line_dim == 1:
        outputs = outputs.transpose(1, 0, 2)
    return outputs


def tri_acts(normed, weights, allowed):
    channels = normed.shape[-1]
    projected = jnp.dot(normed.reshape(-1, channels), weights, preferred_element_type=jnp.float32)
    projected = projected.reshape(normed.shape[0], normed.shape[1], 2 * channels)
    return (
        jax.nn.sigmoid(projected[..., channels:]) * projected[..., :channels] * allowed[..., None]
    ).astype(jnp.bfloat16)


def gather_lines(piece):
    device_count = lax.axis_size("row") * lax.axis_size("col")
    sent = jnp.broadcast_to(piece[None], (device_count,) + piece.shape)
    got = lax.all_to_all(sent, ("row", "col"), 0, 0, tiled=True)
    heads, rows_here, length = piece.shape
    return got.transpose(1, 0, 2, 3).reshape(heads, device_count * rows_here, length)


def shards(
    pair_rep,
    tile_mask,
    chain_ids,
    chain_bias,
    row_project,
    row_bias_proj,
    row_output,
    col_project,
    col_bias_proj,
    col_output,
    tri_left,
    tri_right,
    tri_gate,
    tri_output,
):
    n_row = lax.axis_size("row")
    n_col = lax.axis_size("col")
    device_count = n_row * n_col
    rows_here, length, channels = pair_rep.shape
    head_count = row_bias_proj.shape[1]
    head_size = channels // head_count
    row_index = lax.axis_index("row")
    col_index = lax.axis_index("col")
    device_index = row_index * n_col + col_index
    block_rows = length // n_row
    block_cols = length // n_col
    local_lines = device_index * rows_here + jnp.arange(rows_here, dtype=jnp.int32)
    local_cols = (
        col_index * block_cols + row_index * rows_here + jnp.arange(rows_here, dtype=jnp.int32)
    )
    normed = layer_norm(pair_rep).astype(jnp.bfloat16)
    flat_rows = normed.reshape(rows_here * length, channels)
    bias_rows = jnp.dot(flat_rows, row_bias_proj, preferred_element_type=jnp.float32)
    bias_rows = bias_rows.reshape(rows_here, length, head_count).transpose(2, 0, 1)
    bias_all = gather_lines(bias_rows)
    projected = jnp.dot(flat_rows, row_project, preferred_element_type=jnp.float32).reshape(
        rows_here, length, 4 * channels
    )
    qkv_rows = (
        projected[..., : 3 * channels]
        .astype(jnp.bfloat16)
        .reshape(rows_here, length, 3, head_count, head_size)
    )
    key_ok = tile_rows(local_lines, tile_mask, length)
    mixed_rows = attend_lines(
        qkv_rows[:, :, 0],
        qkv_rows[:, :, 1],
        qkv_rows[:, :, 2],
        projected[..., 3 * channels :],
        bias_all,
        key_ok,
        chain_ids,
        chain_bias[0],
        0,
        False,
    )
    update = jnp.dot(
        mixed_rows.reshape(-1, channels), row_output, preferred_element_type=jnp.float32
    ).reshape(rows_here, length, channels)
    first_pair = (pair_rep.astype(jnp.float32) + update).astype(jnp.bfloat16)
    normed_first = layer_norm(first_pair).astype(jnp.bfloat16)
    bias_next = jnp.dot(
        normed_first.reshape(-1, channels), col_bias_proj, preferred_element_type=jnp.float32
    )
    bias_next = bias_next.reshape(rows_here, length, head_count).transpose(2, 0, 1)
    bias_cols = gather_lines(bias_next)
    first_sent = (
        first_pair.reshape(rows_here, n_col, n_row, rows_here, channels)
        .transpose(0, 2, 1, 3, 4)
        .reshape(rows_here, length, channels)
    )
    columns = lax.all_to_all(first_sent, ("row", "col"), split_axis=1, concat_axis=0, tiled=True)
    normed_cols = layer_norm(columns).astype(jnp.bfloat16)
    projected_cols = jnp.dot(
        normed_cols.reshape(-1, channels), col_project, preferred_element_type=jnp.float32
    ).reshape(length, rows_here, 4 * channels)
    qkv_cols = (
        projected_cols[..., : 3 * channels]
        .astype(jnp.bfloat16)
        .reshape(length, rows_here, 3, head_count, head_size)
    )
    col_ok = tile_rows(local_cols, tile_mask.T, length)
    mixed_cols = attend_lines(
        qkv_cols[:, :, 0],
        qkv_cols[:, :, 1],
        qkv_cols[:, :, 2],
        projected_cols[..., 3 * channels :],
        bias_cols,
        col_ok,
        chain_ids,
        chain_bias[1],
        1,
        True,
    )
    update_cols = jnp.dot(
        mixed_cols.reshape(-1, channels), col_output, preferred_element_type=jnp.float32
    ).reshape(length, rows_here, channels)
    second_pair = (columns.astype(jnp.float32) + update_cols).astype(jnp.bfloat16)
    normed_second = layer_norm(second_pair).astype(jnp.bfloat16)
    edge_mask = tile_pairs(jnp.arange(length, dtype=jnp.int32), local_cols, tile_mask, length)
    left_all = tri_acts(normed_second, tri_left, edge_mask)
    right_all = tri_acts(normed_second, tri_right, edge_mask)
    raw_got = lax.all_to_all(
        second_pair.reshape(n_row, block_rows, rows_here, channels), "row", 0, 0, tiled=True
    )
    own_pair = raw_got.transpose(1, 0, 2, 3).reshape(block_rows, block_cols, channels)
    left_send = jnp.broadcast_to(
        left_all.reshape(n_row, 1, block_rows, rows_here, channels),
        (n_row, n_col, block_rows, rows_here, channels),
    )
    right_send = jnp.broadcast_to(
        right_all.reshape(1, n_col, block_cols, rows_here, channels),
        (n_row, n_col, block_cols, rows_here, channels),
    )
    outgoing = jnp.concatenate([left_send, right_send], axis=2).reshape(
        device_count, block_rows + block_cols, rows_here, channels
    )
    received = lax.all_to_all(outgoing, ("row", "col"), split_axis=0, concat_axis=0, tiled=True)
    product_sum = jnp.einsum(
        "sikc,sjkc->ijc",
        received[:, :block_rows],
        received[:, block_rows:],
        preferred_element_type=jnp.float32,
    )
    normed_own = layer_norm(own_pair).astype(jnp.bfloat16)
    gate_values = jax.nn.sigmoid(
        jnp.dot(normed_own.reshape(-1, channels), tri_gate, preferred_element_type=jnp.float32)
    ).reshape(block_rows, block_cols, channels)
    centered = layer_norm(product_sum).astype(jnp.bfloat16)
    update_tri = jnp.dot(
        centered.reshape(-1, channels), tri_output, preferred_element_type=jnp.float32
    ).reshape(block_rows, block_cols, channels)
    return (own_pair.astype(jnp.float32) + gate_values * update_tri).astype(jnp.bfloat16)


def solution(mesh):
    return jax.shard_map(
        shards,
        mesh=mesh,
        in_specs=(
            P(("row", "col"), None, None),
            P(),
            P(),
            P(),
            P(),
            P(),
            P(),
            P(),
            P(),
            P(),
            P(),
            P(),
            P(),
            P(),
        ),
        out_specs=P("row", "col", None),
        check_vma=False,
    )
```

profile of v0, /device:TPU:1, one launch (start us, length us, event | category | flops | bytes accessed | tf_op | source)
XLA Modules:
  0.0 142.1 jit_solution(1615348873690497271)
XLA Ops:
  0.0 1.1 convert_reduce_fusion
  1.1 1.1 fusion.48
  2.2 1.2 convolution_bitcast_fusion.2
  3.5 0.7 broadcast_in_dim.69
  4.2 7.1 %all-to-all-start = ((f32[32,4,4,128]{3,2,1,0:T(4,128)}), f32[32,4,4,128]{3,2,1,0:T(4,128)S(1)}, u32[]{:S(2)}, u32[]{:S(2)}) async-start(f32[32,4,4,128]{3,2,1,0:T(4,128)} %broadcast_in_dim.69), calls=%async_computation | async-start | bytes 524288 | tf_op jit(solution)/shard_map/all_to_all | solution.py:110
  12.0 1.3 fusion.70
  13.8 7.8 %all-to-all-done = f32[32,4,4,128]{3,2,1,0:T(4,128)S(1)} async-done(((f32[32,4,4,128]{3,2,1,0:T(4,128)}), f32[32,4,4,128]{3,2,1,0:T(4,128)S(1)}, u32[]{:S(2)}, u32[]{:S(2)}) %all-to-all-start) | async-done | bytes 262176 | tf_op jit(solution)/shard_map/all_to_all | solution.py:110
  21.9 14.2 %while.24 = (s32[]{:T(128)}, bf16[4,128,128]{1,2,0:T(8,128)(2,1)S(1)}, s32[4]{0:T(128)S(1)}, bf16[4,128,4,32]{1,3,2,0:T(8,128)(2,1)S(1)}, pred[4,128]{1,0:T(4,12...) while((s32[]{:T(128)}, ...), condition=%wide.region_5.6_spmd, body=%wide.region_2.5_spmd.sunk | while | flops 9159427 | bytes 2038723 | solution.py:91
  36.8 0.8 copy.147
  37.6 2.6 %all-to-all-start.1 = ((bf16[4,128,128]{2,0,1:T(4,128)(2,1)}), bf16[4,128,128]{2,0,1:T(4,128)(2,1)S(1)}, u32[]{:S(2)}, u32[]{:S(2)}) async-start(bf16[4,128,128]{2,0,1:T(4,128)(2,1)} %copy.147), calls=%async_computation.1 | async-start | bytes 262144 | tf_op jit(solution)/shard_map/all_to_all | solution.py:187
  40.5 7.0 %all-to-all-done.1 = bf16[4,128,128]{2,0,1:T(4,128)(2,1)S(1)} async-done(((bf16[4,128,128]{2,0,1:T(4,128)(2,1)}), bf16[4,128,128]{2,0,1:T(4,128)(2,1)S(1)}, u32[]{:S(2)}, u32[]{:S(2)}) %all-to-all-start.1) | async-done | bytes 131104 | tf_op jit(solution)/shard_map/all_to_all | solution.py:187
  48.3 3.5 %all-to-all-start.2 = ((f32[32,4,4,128]{3,2,1,0:T(4,128)}), f32[32,4,4,128]{3,2,1,0:T(4,128)S(1)}, u32[]{:S(2)}, u32[]{:S(2)}) async-start(f32[32,4,4,128]{3,2,1,0:T(4,128)} %broadcast_in_dim.70), calls=%async_computation.2 | async-start | bytes 524288 | tf_op jit(solution)/shard_map/all_to_all | solution.py:110
  54.3 7.9 %all-to-all-done.2 = f32[32,4,4,128]{3,2,1,0:T(4,128)S(1)} async-done(((f32[32,4,4,128]{3,2,1,0:T(4,128)}), f32[32,4,4,128]{3,2,1,0:T(4,128)S(1)}, u32[]{:S(2)}, u32[]{:S(2)}) %all-to-all-start.2) | async-done | bytes 262176 | tf_op jit(solution)/shard_map/all_to_all | solution.py:110
  62.4 13.3 %while.25 = (s32[]{:T(128)}, bf16[4,128,128]{1,2,0:T(8,128)(2,1)S(1)}, s32[4]{0:T(128)S(1)}, bf16[128,4,4,32]{0,3,2,1:T(8,128)(2,1)S(1)}, pred[4,128]{1,0:T(4,12...) while((s32[]{:T(128)}, ...), condition=%wide.region_13.14_spmd, body=%wide.region_10.13_spmd.sunk | while | flops 9159427 | bytes 2038723 | solution.py:91
  77.2 0.8 copy.160
  78.0 3.4 %all-to-all-start.3 = ((bf16[8,16,4,128]{3,2,1,0:T(4,128)(2,1)}), bf16[8,16,4,128]{3,2,1,0:T(4,128)(2,1)S(1)}, u32[]{:S(2)}, u32[]{:S(2)}) async-start(bf16[8,16,4,128]{3,2,1,0:T(4,128)(2,1)} %copy.160), calls=%async_computation.3 | async-start | bytes 262144 | tf_op jit(solution)/shard_map/all_to_all | solution.py:218
  81.8 1.3 pad_maximum_fusion
  83.1 2.9 %all-to-all-done.3 = bf16[8,16,4,128]{3,2,1,0:T(4,128)(2,1)S(1)} async-done(((bf16[8,16,4,128]{3,2,1,0:T(4,128)(2,1)}), bf16[8,16,4,128]{3,2,1,0:T(4,128)(2,1)S(1)}, u32[]{:S(2)}, u32[]{:S(2)}) %all-to-all-start.3) | async-done | bytes 131104 | tf_op jit(solution)/shard_map/all_to_all | solution.py:218
  86.0 3.4 %all-to-all-start.4 = ((bf16[32,48,4,128]{3,1,2,0:T(8,128)(2,1)}), bf16[32,48,4,128]{3,1,2,0:T(8,128)(2,1)S(1)}, u32[]{:S(2)}, u32[]{:S(2)}) async-start(bf16[32,48,4,128]{3,1,2,0:T(8,128)(2,1)} %bitcast.57), calls=%async_computation.4 | async-start | bytes 3145728 | tf_op jit(solution)/shard_map/all_to_all | solution.py:233
  91.4 35.6 %all-to-all-done.4 = bf16[32,48,4,128]{3,1,2,0:T(8,128)(2,1)S(1)} async-done(((bf16[32,48,4,128]{3,1,2,0:T(8,128)(2,1)}), bf16[32,48,4,128]{3,1,2,0:T(8,128)(2,1)S(1)}, u32[]{:S(2)}, u32[]{:S(2)}) %all-to-all-start.4) | async-done | bytes 1572896 | tf_op jit(solution)/shard_map/all_to_all | solution.py:233
  127.0 6.4 %copy.181 = bf16[32,32,4,128]{1,0,2,3:T(8,128)(2,1)} copy(bf16[32,32,4,128]{3,1,2,0:T(8,128)(2,1)S(1)} %slice.89) | data formatting | bytes 2097152
  133.4 3.2 %copy.180 = bf16[32,16,4,128]{0,1,2,3:T(8,128)(2,1)S(1)} copy(bf16[32,16,4,128]{3,1,2,0:T(8,128)(2,1)S(1)} %slice.88) | data formatting | bytes 1048576
  136.7 3.7 %fusion.97 = (f32[16,32]{1,0:T(8,128)S(1)}, f32[16,32,128]{1,0,2:T(8,128)S(1)}) fusion(bf16[32,16,4,128]{0,1,2,3:T(8,128)(2,1)S(1)} %copy.180, bf16[32,32,4,128]{1,0,2,3:T(8,128)(2,1)} %copy.181), kind=kOutput, calls=%fused_computation.169 | convolution fusion | flops 16842240 | bytes 1837056 | tf_op jit(solution)/shard_map/sikc,sjkc->ijc/dot_general | solution.py:234
  141.2 1.0 fusion.40
  (173 shorter events, 20.7 us)
Async XLA Ops:
  0.0 12.0 %copy-start = (bf16[128,512]{1,0:T(8,128)(2,1)S(1)}, bf16[128,512]{1,0:T(8,128)(2,1)}, u32[]{:S(2)}) copy-start(bf16[128,512]{1,0:T(8,128)(2,1)} %param.22) | copy-start | bytes 393220
  0.0 13.3 %copy-start.9 = (f32[2,4]{1,0:T(2,128)S(1)}, f32[2,4]{1,0:T(2,128)}, u32[]{:S(2)}) copy-start(f32[2,4]{1,0:T(2,128)} %param.21) | copy-start | bytes 100
  4.2 17.4 %all-to-all-start = ((f32[32,4,4,128]{3,2,1,0:T(4,128)}), f32[32,4,4,128]{3,2,1,0:T(4,128)S(1)}, u32[]{:S(2)}, u32[]{:S(2)}) async-start(f32[32,4,4,128]{3,2,1,0:T(4,128)} %broadcast_in_dim.69), calls=%async_computation | async-start | bytes 524288 | tf_op jit(solution)/shard_map/all_to_all | solution.py:110
  13.3 8.6 %copy-start.2 = (s32[128]{0:T(128)S(1)}, s32[128]{0:T(128)}, u32[]{:S(2)}) copy-start(s32[128]{0:T(128)} %param.20) | copy-start | bytes 1540
  21.9 14.2 %copy-start.1 = (bf16[4,128,128]{2,1,0:T(8,128)(2,1)S(1)}, bf16[4,128,128]{2,1,0:T(8,128)(2,1)}, u32[]{:S(2)}) copy-start(bf16[4,128,128]{2,1,0:T(8,128)(2,1)} %param.18) | copy-start | bytes 393220
  21.9 14.2 %copy-start.8 = (bf16[128,128]{1,0:T(8,128)(2,1)S(1)}, bf16[128,128]{1,0:T(8,128)(2,1)}, u32[]{:S(2)}) copy-start(bf16[128,128]{1,0:T(8,128)(2,1)} %param.24) | copy-start | bytes 98308
  21.9 18.3 %copy-start.11 = (bf16[128,4]{0,1:T(4,128)(2,1)S(1)}, bf16[128,4]{0,1:T(4,128)(2,1)}, u32[]{:S(2)}) copy-start(bf16[128,4]{0,1:T(4,128)(2,1)} %param.26) | copy-start | bytes 3076
  36.8 16.7 %copy-start.3 = (bf16[128,512]{1,0:T(8,128)(2,1)S(1)}, bf16[128,512]{1,0:T(8,128)(2,1)}, u32[]{:S(2)}) copy-start(bf16[128,512]{1,0:T(8,128)(2,1)} %param.25) | copy-start | bytes 393220
  37.6 9.9 %all-to-all-start.1 = ((bf16[4,128,128]{2,0,1:T(4,128)(2,1)}), bf16[4,128,128]{2,0,1:T(4,128)(2,1)S(1)}, u32[]{:S(2)}, u32[]{:S(2)}) async-start(bf16[4,128,128]{2,0,1:T(4,128)(2,1)} %copy.147), calls=%async_computation.1 | async-start | bytes 262144 | tf_op jit(solution)/shard_map/all_to_all | solution.py:187
  48.3 13.9 %all-to-all-start.2 = ((f32[32,4,4,128]{3,2,1,0:T(4,128)}), f32[32,4,4,128]{3,2,1,0:T(4,128)S(1)}, u32[]{:S(2)}, u32[]{:S(2)}) async-start(f32[32,4,4,128]{3,2,1,0:T(4,128)} %broadcast_in_dim.70), calls=%async_computation.2 | async-start | bytes 524288 | tf_op jit(solution)/shard_map/all_to_all | solution.py:110
  62.3 13.4 %copy-start.6 = (bf16[128,128]{1,0:T(8,128)(2,1)S(1)}, bf16[128,128]{1,0:T(8,128)(2,1)}, u32[]{:S(2)}) copy-start(bf16[128,128]{1,0:T(8,128)(2,1)} %param.27) | copy-start | bytes 98308
  62.3 14.0 %copy-start.4 = (bf16[128,256]{1,0:T(8,128)(2,1)S(1)}, bf16[128,256]{1,0:T(8,128)(2,1)}, u32[]{:S(2)}) copy-start(bf16[128,256]{1,0:T(8,128)(2,1)} %param.29) | copy-start | bytes 196612
  62.4 14.3 %copy-start.5 = (bf16[128,256]{1,0:T(8,128)(2,1)S(1)}, bf16[128,256]{1,0:T(8,128)(2,1)}, u32[]{:S(2)}) copy-start(bf16[128,256]{1,0:T(8,128)(2,1)} %param.28) | copy-start | bytes 196612
  78.0 8.0 %all-to-all-start.3 = ((bf16[8,16,4,128]{3,2,1,0:T(4,128)(2,1)}), bf16[8,16,4,128]{3,2,1,0:T(4,128)(2,1)S(1)}, u32[]{:S(2)}, u32[]{:S(2)}) async-start(bf16[8,16,4,128]{3,2,1,0:T(4,128)(2,1)} %copy.160), calls=%async_computation.3 | async-start | bytes 262144 | tf_op jit(solution)/shard_map/all_to_all | solution.py:218
  86.0 5.0 %copy-start.10 = (bf16[128,128]{1,0:T(8,128)(2,1)S(1)}, bf16[128,128]{1,0:T(8,128)(2,1)}, u32[]{:S(2)}) copy-start(bf16[128,128]{1,0:T(8,128)(2,1)} %param.30) | copy-start | bytes 98308
  86.0 40.9 %all-to-all-start.4 = ((bf16[32,48,4,128]{3,1,2,0:T(8,128)(2,1)}), bf16[32,48,4,128]{3,1,2,0:T(8,128)(2,1)S(1)}, u32[]{:S(2)}, u32[]{:S(2)}) async-start(bf16[32,48,4,128]{3,1,2,0:T(8,128)(2,1)} %bitcast.57), calls=%async_computation.4 | async-start | bytes 3145728 | tf_op jit(solution)/shard_map/all_to_all | solution.py:233
  140.4 0.8 copy-start.7
where the time goes:
time: 143 us; the launch traced here: 142 us
  waiting for transfers between devices  61.3 us (43%)
  local copies, waits for them, and re-layouts  22.5 us (16%)
  starting transfers between devices  19.9 us (14%)
  loops' own time  16.5 us (12%)
  matrix products  13 us (9%)
  other arithmetic  7.65 us (5%)
    all_to_all x1, waiting for transfers between devices, shards(): lax.all_to_all(outgoing, ('row', 'col'), split_axis=0, concat_axis=0, til...  35.6 us
    another operation x2, loops' own time, attend_lines(): lax.map(one_block, jnp.arange(line_count * per_line, dtype=jnp.int32))  16.5 us
    all_to_all x2, waiting for transfers between devices, gather_lines(): got = lax.all_to_all(sent, ('row', 'col'), 0, 0, tiled=True)  15.8 us
    all_to_all x2, starting transfers between devices, gather_lines(): got = lax.all_to_all(sent, ('row', 'col'), 0, 0, tiled=True)  10.5 us
    unnamed x26, local copies, waits for them, and re-layouts  10.1 us
    all_to_all x1, waiting for transfers between devices, shards(): lax.all_to_all(first_sent, ('row', 'col'), split_axis=1, concat_axis=0, t...  7.03 us
    dynamic_slice x8, local copies, waits for them, and re-layouts, attend_lines(): lax.map(one_block, jnp.arange(line_count * per_line, dtype=jnp.int32))  5.01 us
    dot_general x1, matrix products, shards(): jnp.einsum('sikc,sjkc->ijc', received[:, :block_rows], received[:, block_...  3.72 us
  transfers between devices with their start and end apart: 5, of which 5 were waited for; matrix products, arithmetic and copies ran while one was open for 6% of the time, Pallas kernels for 0%

commit v1 on v0

--- a/solution.py
+++ b/solution.py
@@ -2,6 +2,22 @@
 import jax.numpy as jnp
 from jax import lax
 from jax.sharding import PartitionSpec as P
+
+
+def exchange_in_pairs(value, axis, split, join):
+    ways, here = (lax.axis_size(axis), lax.axis_index(axis))
+    width = value.shape[split] // ways
+    dims = list(value.shape)
+    dims[split] = width
+    height = dims[join]
+    dims[join] = height * ways
+    full = jnp.zeros(dims, value.dtype)
+    for mask in range(ways):
+        part = lax.dynamic_slice_in_dim(value, (here ^ mask) * width, width, axis=split)
+        if mask:
+            part = lax.ppermute(part, axis, [(d, d ^ mask) for d in range(ways)])
+        full = lax.dynamic_update_slice_in_dim(full, part, (here ^ mask) * height, axis=join)
+    return full
 
 
 def layer_norm(values):
@@ -215,8 +231,8 @@
     edge_mask = tile_pairs(jnp.arange(length, dtype=jnp.int32), local_cols, tile_mask, length)
     left_all = tri_acts(normed_second, tri_left, edge_mask)
     right_all = tri_acts(normed_second, tri_right, edge_mask)
-    raw_got = lax.all_to_all(
-        second_pair.reshape(n_row, block_rows, rows_here, channels), "row", 0, 0, tiled=True
+    raw_got = exchange_in_pairs(
+        second_pair.reshape(n_row, block_rows, rows_here, channels), "row", 0, 0
     )
     own_pair = raw_got.transpose(1, 0, 2, 3).reshape(block_rows, block_cols, channels)
     left_send = jnp.broadcast_to(

time: 143 us -> 135 us (0.944)
  waiting for transfers between devices: 61.3 us -> 49.7 us
  starting transfers between devices: 19.9 us -> 24.7 us
    all_to_all x1, waiting for transfers between devices: 35.6 us -> 21 us  [shards(): lax.all_to_all(outgoing, ('row', 'col'), split_axis=0, concat_axis=0, til...]
    ppermute x0 -> x7, starting transfers between devices: none -> 8.9 us  [exchange_in_pairs(): part = lax.ppermute(part, axis, [(d, d ^ mask) for d in range(ways)])]
    ppermute x0 -> x7, waiting for transfers between devices: none -> 5.92 us  [exchange_in_pairs(): part = lax.ppermute(part, axis, [(d, d ^ mask) for d in range(ways)])]
    all_to_all x1 -> x0, starting transfers between devices: 3.44 us -> none  [shards(): lax.all_to_all(second_pair.reshape(n_row, block_rows, rows_here, channels...]
    all_to_all x1 -> x0, waiting for transfers between devices: 2.92 us -> none  [shards(): lax.all_to_all(second_pair.reshape(n_row, block_rows, rows_here, channels...]
  transfers between devices with their start and end apart: 5 -> 11, of which waited for: 5 -> 7; matrix products, arithmetic and copies ran while one was open for 6% -> 4% of each run, Pallas kernels for 0% -> 0%
where the time goes in v1:
time: 135 us; the launch traced here: 134 us
  waiting for transfers between devices  49.7 us (37%)
  starting transfers between devices  24.7 us (18%)
  local copies, waits for them, and re-layouts  21.3 us (16%)
  loops' own time  16.5 us (12%)
  matrix products  12.3 us (9%)
  other arithmetic  8.35 us (6%)
    all_to_all x1, waiting for transfers between devices, shards(): lax.all_to_all(outgoing, ('row', 'col'), split_axis=0, concat_axis=0, til...  21 us
    another operation x2, loops' own time, attend_lines(): lax.map(one_block, jnp.arange(line_count * per_line, dtype=jnp.int32))  16.5 us
    all_to_all x2, waiting for transfers between devices, gather_lines(): got = lax.all_to_all(sent, ('row', 'col'), 0, 0, tiled=True)  15.8 us
    all_to_all x2, starting transfers between devices, gather_lines(): got = lax.all_to_all(sent, ('row', 'col'), 0, 0, tiled=True)  10.5 us
    unnamed x26, local copies, waits for them, and re-layouts  10.1 us
    ppermute x7, starting transfers between devices, exchange_in_pairs(): part = lax.ppermute(part, axis, [(d, d ^ mask) for d in range(ways)])  8.9 us
    all_to_all x1, waiting for transfers between devices, shards(): lax.all_to_all(first_sent, ('row', 'col'), split_axis=1, concat_axis=0, t...  7.03 us
    ppermute x7, waiting for transfers between devices, exchange_in_pairs(): part = lax.ppermute(part, axis, [(d, d ^ mask) for d in range(ways)])  5.92 us
  transfers between devices with their start and end apart: 11, of which 7 were waited for; matrix products, arithmetic and copies ran while one was open for 4% of the time, Pallas kernels for 0%

profile of v1, /device:TPU:1, one launch (start us, length us, event | category | flops | bytes accessed | tf_op | source)
XLA Modules:
  0.0 134.3 jit_solution(12388107856718237065)
XLA Ops:
  0.0 1.1 convert_reduce_fusion
  1.1 1.1 fusion.46
  2.2 1.2 convolution_bitcast_fusion.2
  4.2 7.1 %all-to-all-start = ((f32[32,4,4,128]{3,2,1,0:T(4,128)}), f32[32,4,4,128]{3,2,1,0:T(4,128)S(1)}, u32[]{:S(2)}, u32[]{:S(2)}) async-start(f32[32,4,4,128]{3,2,1,0:T(4,128)} %broadcast_in_dim.72), calls=%async_computation | async-start | bytes 524288 | tf_op jit(solution)/shard_map/all_to_all | solution.py:126
  12.0 1.3 fusion.69
  13.7 7.9 %all-to-all-done = f32[32,4,4,128]{3,2,1,0:T(4,128)S(1)} async-done(((f32[32,4,4,128]{3,2,1,0:T(4,128)}), f32[32,4,4,128]{3,2,1,0:T(4,128)S(1)}, u32[]{:S(2)}, u32[]{:S(2)}) %all-to-all-start) | async-done | bytes 262176 | tf_op jit(solution)/shard_map/all_to_all | solution.py:126
  21.9 14.2 %while.24 = (s32[]{:T(128)}, bf16[4,128,128]{1,2,0:T(8,128)(2,1)S(1)}, s32[4]{0:T(128)S(1)}, bf16[4,128,4,32]{1,3,2,0:T(8,128)(2,1)S(1)}, pred[4,128]{1,0:T(4,12...) while((s32[]{:T(128)}, ...), condition=%wide.region_5.6_spmd, body=%wide.region_2.5_spmd.sunk | while | flops 9159427 | bytes 2038723 | solution.py:107
  37.6 2.6 %all-to-all-start.1 = ((bf16[4,128,128]{2,0,1:T(4,128)(2,1)}), bf16[4,128,128]{2,0,1:T(4,128)(2,1)S(1)}, u32[]{:S(2)}, u32[]{:S(2)}) async-start(bf16[4,128,128]{2,0,1:T(4,128)(2,1)} %copy.140), calls=%async_computation.1 | async-start | bytes 262144 | tf_op jit(solution)/shard_map/all_to_all | solution.py:203
  40.5 7.0 %all-to-all-done.1 = bf16[4,128,128]{2,0,1:T(4,128)(2,1)S(1)} async-done(((bf16[4,128,128]{2,0,1:T(4,128)(2,1)}), bf16[4,128,128]{2,0,1:T(4,128)(2,1)S(1)}, u32[]{:S(2)}, u32[]{:S(2)}) %all-to-all-start.1) | async-done | bytes 131104 | tf_op jit(solution)/shard_map/all_to_all | solution.py:203
  48.3 3.5 %all-to-all-start.2 = ((f32[32,4,4,128]{3,2,1,0:T(4,128)}), f32[32,4,4,128]{3,2,1,0:T(4,128)S(1)}, u32[]{:S(2)}, u32[]{:S(2)}) async-start(f32[32,4,4,128]{3,2,1,0:T(4,128)} %broadcast_in_dim.73), calls=%async_computation.2 | async-start | bytes 524288 | tf_op jit(solution)/shard_map/all_to_all | solution.py:126
  54.2 7.9 %all-to-all-done.2 = f32[32,4,4,128]{3,2,1,0:T(4,128)S(1)} async-done(((f32[32,4,4,128]{3,2,1,0:T(4,128)}), f32[32,4,4,128]{3,2,1,0:T(4,128)S(1)}, u32[]{:S(2)}, u32[]{:S(2)}) %all-to-all-start.2) | async-done | bytes 262176 | tf_op jit(solution)/shard_map/all_to_all | solution.py:126
  62.4 13.3 %while.25 = (s32[]{:T(128)}, bf16[4,128,128]{1,2,0:T(8,128)(2,1)S(1)}, s32[4]{0:T(128)S(1)}, bf16[128,4,4,32]{0,3,2,1:T(8,128)(2,1)S(1)}, pred[4,128]{1,0:T(4,12...) while((s32[]{:T(128)}, ...), condition=%wide.region_13.14_spmd, body=%wide.region_10.13_spmd.sunk | while | flops 9159427 | bytes 2038723 | solution.py:107
  77.6 1.3 pad_maximum_fusion
  78.9 2.7 %all-to-all-start.3 = ((bf16[32,48,4,128]{3,1,2,0:T(8,128)(2,1)}), bf16[32,48,4,128]{3,1,2,0:T(8,128)(2,1)S(1)}, u32[]{:S(2)}, u32[]{:S(2)}) async-start(bf16[32,48,4,128]{3,1,2,0:T(8,128)(2,1)} %bitcast.57), calls=%async_computation.3 | async-start | bytes 3145728 | tf_op jit(solution)/shard_map/all_to_all | solution.py:249
  82.2 1.2 collective-permute-start.1
  83.9 1.2 collective-permute-start.3
  85.8 2.2 %collective-permute-start.5 = (bf16[1,16,4,128]{3,1,0,2:T(8,128)(2,1)S(1)}, bf16[1,16,4,128]{3,1,0,2:T(8,128)(2,1)S(1)}, u32[]{:S(2)}, u32[]{:S(2)}) collective-permute-start(bf16[1,16,4,128]{3,1,0,2:T(8,128)(2,1)S(1)} %get-tuple-element.446), channel_id=1, source_target_pairs={{0,24},{4,28},{8,16},{12,20},{16,8},{20,12},{24,0},{28,4},{1,25},{... | collective-permute-start | bytes 49160 | tf_op jit(solution)/shard_map/ppermute | solution.py:18
  88.0 3.9 %collective-permute-done.1 = bf16[1,16,4,128]{3,1,0,2:T(8,128)(2,1)S(1)} collective-permute-done((bf16[1,16,4,128]{3,1,0,2:T(8,128)(2,1)S(1)}, bf16[1,16,4,128]{3,1,0,2:T(8,128)(2,1)S(1)}, u32[]{:S(2)}, u32[]{:S(2)}) %collective-permute-start.1) | collective-permute-done | bytes 16416 | tf_op jit(solution)/shard_map/ppermute | solution.py:18
  91.9 2.7 %collective-permute-start.6 = (bf16[1,16,4,128]{3,1,0,2:T(8,128)(2,1)S(1)}, bf16[1,16,4,128]{3,1,0,2:T(8,128)(2,1)S(1)}, u32[]{:S(2)}, u32[]{:S(2)}) collective-permute-start(bf16[1,16,4,128]{3,1,0,2:T(8,128)(2,1)S(1)} %get-tuple-element.445), channel_id=1, source_target_pairs={{0,28},{4,24},{8,20},{12,16},{16,12},{20,8},{24,4},{28,0},{1,29},{... | collective-permute-start | bytes 49160 | tf_op jit(solution)/shard_map/ppermute | solution.py:18
  94.8 1.2 collective-permute-done.4
  98.0 21.0 %all-to-all-done.3 = bf16[32,48,4,128]{3,1,2,0:T(8,128)(2,1)S(1)} async-done(((bf16[32,48,4,128]{3,1,2,0:T(8,128)(2,1)}), bf16[32,48,4,128]{3,1,2,0:T(8,128)(2,1)S(1)}, u32[]{:S(2)}, u32[]{:S(2)}) %all-to-all-start.3) | async-done | bytes 1572896 | tf_op jit(solution)/shard_map/all_to_all | solution.py:249
  119.1 6.4 %copy.174 = bf16[32,32,4,128]{1,0,2,3:T(8,128)(2,1)} copy(bf16[32,32,4,128]{3,1,2,0:T(8,128)(2,1)S(1)} %slice.89) | data formatting | bytes 2097152
  125.5 3.2 %copy.173 = bf16[32,16,4,128]{0,1,2,3:T(8,128)(2,1)S(1)} copy(bf16[32,16,4,128]{3,1,2,0:T(8,128)(2,1)S(1)} %slice.88) | data formatting | bytes 1048576
  128.8 3.7 %fusion.96 = (f32[16,32]{1,0:T(8,128)S(1)}, f32[16,32,128]{1,0,2:T(8,128)S(1)}) fusion(bf16[32,16,4,128]{0,1,2,3:T(8,128)(2,1)S(1)} %copy.173, bf16[32,32,4,128]{1,0,2,3:T(8,128)(2,1)} %copy.174), kind=kOutput, calls=%fused_computation.185 | convolution fusion | flops 16842240 | bytes 1837056 | tf_op jit(solution)/shard_map/sikc,sjkc->ijc/dot_general | solution.py:250
  (188 shorter events, 25.1 us)
Async XLA Ops:
  0.0 12.0 %copy-start = (bf16[128,512]{1,0:T(8,128)(2,1)S(1)}, bf16[128,512]{1,0:T(8,128)(2,1)}, u32[]{:S(2)}) copy-start(bf16[128,512]{1,0:T(8,128)(2,1)} %param.22) | copy-start | bytes 393220
  0.0 13.3 %copy-start.9 = (f32[2,4]{1,0:T(2,128)S(1)}, f32[2,4]{1,0:T(2,128)}, u32[]{:S(2)}) copy-start(f32[2,4]{1,0:T(2,128)} %param.21) | copy-start | bytes 100
  4.2 17.4 %all-to-all-start = ((f32[32,4,4,128]{3,2,1,0:T(4,128)}), f32[32,4,4,128]{3,2,1,0:T(4,128)S(1)}, u32[]{:S(2)}, u32[]{:S(2)}) async-start(f32[32,4,4,128]{3,2,1,0:T(4,128)} %broadcast_in_dim.72), calls=%async_computation | async-start | bytes 524288 | tf_op jit(solution)/shard_map/all_to_all | solution.py:126
  13.3 8.6 %copy-start.2 = (s32[128]{0:T(128)S(1)}, s32[128]{0:T(128)}, u32[]{:S(2)}) copy-start(s32[128]{0:T(128)} %param.20) | copy-start | bytes 1540
  21.9 14.2 %copy-start.1 = (bf16[4,128,128]{2,1,0:T(8,128)(2,1)S(1)}, bf16[4,128,128]{2,1,0:T(8,128)(2,1)}, u32[]{:S(2)}) copy-start(bf16[4,128,128]{2,1,0:T(8,128)(2,1)} %param.18) | copy-start | bytes 393220
  21.9 14.2 %copy-start.8 = (bf16[128,128]{1,0:T(8,128)(2,1)S(1)}, bf16[128,128]{1,0:T(8,128)(2,1)}, u32[]{:S(2)}) copy-start(bf16[128,128]{1,0:T(8,128)(2,1)} %param.24) | copy-start | bytes 98308
  21.9 18.3 %copy-start.11 = (bf16[128,4]{0,1:T(4,128)(2,1)S(1)}, bf16[128,4]{0,1:T(4,128)(2,1)}, u32[]{:S(2)}) copy-start(bf16[128,4]{0,1:T(4,128)(2,1)} %param.26) | copy-start | bytes 3076
  36.8 16.7 %copy-start.3 = (bf16[128,512]{1,0:T(8,128)(2,1)S(1)}, bf16[128,512]{1,0:T(8,128)(2,1)}, u32[]{:S(2)}) copy-start(bf16[128,512]{1,0:T(8,128)(2,1)} %param.25) | copy-start | bytes 393220
  37.6 9.9 %all-to-all-start.1 = ((bf16[4,128,128]{2,0,1:T(4,128)(2,1)}), bf16[4,128,128]{2,0,1:T(4,128)(2,1)S(1)}, u32[]{:S(2)}, u32[]{:S(2)}) async-start(bf16[4,128,128]{2,0,1:T(4,128)(2,1)} %copy.140), calls=%async_computation.1 | async-start | bytes 262144 | tf_op jit(solution)/shard_map/all_to_all | solution.py:203
  48.3 13.9 %all-to-all-start.2 = ((f32[32,4,4,128]{3,2,1,0:T(4,128)}), f32[32,4,4,128]{3,2,1,0:T(4,128)S(1)}, u32[]{:S(2)}, u32[]{:S(2)}) async-start(f32[32,4,4,128]{3,2,1,0:T(4,128)} %broadcast_in_dim.73), calls=%async_computation.2 | async-start | bytes 524288 | tf_op jit(solution)/shard_map/all_to_all | solution.py:126
  62.3 13.4 %copy-start.6 = (bf16[128,128]{1,0:T(8,128)(2,1)S(1)}, bf16[128,128]{1,0:T(8,128)(2,1)}, u32[]{:S(2)}) copy-start(bf16[128,128]{1,0:T(8,128)(2,1)} %param.27) | copy-start | bytes 98308
  62.3 14.0 %copy-start.4 = (bf16[128,256]{1,0:T(8,128)(2,1)S(1)}, bf16[128,256]{1,0:T(8,128)(2,1)}, u32[]{:S(2)}) copy-start(bf16[128,256]{1,0:T(8,128)(2,1)} %param.29) | copy-start | bytes 196612
  62.4 14.3 %copy-start.5 = (bf16[128,256]{1,0:T(8,128)(2,1)S(1)}, bf16[128,256]{1,0:T(8,128)(2,1)}, u32[]{:S(2)}) copy-start(bf16[128,256]{1,0:T(8,128)(2,1)} %param.28) | copy-start | bytes 196612
  78.9 18.8 %copy-start.10 = (bf16[128,128]{1,0:T(8,128)(2,1)S(1)}, bf16[128,128]{1,0:T(8,128)(2,1)}, u32[]{:S(2)}) copy-start(bf16[128,128]{1,0:T(8,128)(2,1)} %param.30) | copy-start | bytes 98308
  78.9 40.1 %all-to-all-start.3 = ((bf16[32,48,4,128]{3,1,2,0:T(8,128)(2,1)}), bf16[32,48,4,128]{3,1,2,0:T(8,128)(2,1)S(1)}, u32[]{:S(2)}, u32[]{:S(2)}) async-start(bf16[32,48,4,128]{3,1,2,0:T(8,128)(2,1)} %bitcast.57), calls=%async_computation.3 | async-start | bytes 3145728 | tf_op jit(solution)/shard_map/all_to_all | solution.py:249
  81.7 4.1 %collective-permute-start = (bf16[1,16,4,128]{3,1,0,2:T(8,128)(2,1)S(1)}, bf16[1,16,4,128]{3,1,0,2:T(8,128)(2,1)S(1)}, u32[]{:S(2)}, u32[]{:S(2)}) collective-permute-start(bf16[1,16,4,128]{3,1,0,2:T(8,128)(2,1)S(1)} %get-tuple-element.451), channel_id=1, source_target_pairs={{0,4},{4,0},{8,12},{12,8},{16,20},{20,16},{24,28},{28,24},{1,5},{5... | collective-permute-start | bytes 49160 | tf_op jit(solution)/shard_map/ppermute | solution.py:18
  82.2 9.7 %collective-permute-start.1 = (bf16[1,16,4,128]{3,1,0,2:T(8,128)(2,1)S(1)}, bf16[1,16,4,128]{3,1,0,2:T(8,128)(2,1)S(1)}, u32[]{:S(2)}, u32[]{:S(2)}) collective-permute-start(bf16[1,16,4,128]{3,1,0,2:T(8,128)(2,1)S(1)} %get-tuple-element.450), channel_id=1, source_target_pairs={{0,8},{4,12},{8,0},{12,4},{16,24},{20,28},{24,16},{28,20},{1,9},{5... | collective-permute-start | bytes 49160 | tf_op jit(solution)/shard_map/ppermute | solution.py:18
  83.4 11.3 %collective-permute-start.2 = (bf16[1,16,4,128]{3,1,0,2:T(8,128)(2,1)S(1)}, bf16[1,16,4,128]{3,1,0,2:T(8,128)(2,1)S(1)}, u32[]{:S(2)}, u32[]{:S(2)}) collective-permute-start(bf16[1,16,4,128]{3,1,0,2:T(8,128)(2,1)S(1)} %get-tuple-element.449), channel_id=1, source_target_pairs={{0,12},{4,8},{8,4},{12,0},{16,28},{20,24},{24,20},{28,16},{1,13},{... | collective-permute-start | bytes 49160 | tf_op jit(solution)/shard_map/ppermute | solution.py:18
  83.9 10.8 %collective-permute-start.3 = (bf16[1,16,4,128]{3,1,0,2:T(8,128)(2,1)S(1)}, bf16[1,16,4,128]{3,1,0,2:T(8,128)(2,1)S(1)}, u32[]{:S(2)}, u32[]{:S(2)}) collective-permute-start(bf16[1,16,4,128]{3,1,0,2:T(8,128)(2,1)S(1)} %get-tuple-element.448), channel_id=1, source_target_pairs={{0,16},{4,20},{8,24},{12,28},{16,0},{20,4},{24,8},{28,12},{1,17},{... | collective-permute-start | bytes 49160 | tf_op jit(solution)/shard_map/ppermute | solution.py:18
  85.2 10.8 %collective-permute-start.4 = (bf16[1,16,4,128]{3,1,0,2:T(8,128)(2,1)S(1)}, bf16[1,16,4,128]{3,1,0,2:T(8,128)(2,1)S(1)}, u32[]{:S(2)}, u32[]{:S(2)}) collective-permute-start(bf16[1,16,4,128]{3,1,0,2:T(8,128)(2,1)S(1)} %get-tuple-element.447), channel_id=1, source_target_pairs={{0,20},{4,16},{8,28},{12,24},{16,4},{20,0},{24,12},{28,8},{1,21},{... | collective-permute-start | bytes 49160 | tf_op jit(solution)/shard_map/ppermute | solution.py:18
  85.8 10.2 %collective-permute-start.5 = (bf16[1,16,4,128]{3,1,0,2:T(8,128)(2,1)S(1)}, bf16[1,16,4,128]{3,1,0,2:T(8,128)(2,1)S(1)}, u32[]{:S(2)}, u32[]{:S(2)}) collective-permute-start(bf16[1,16,4,128]{3,1,0,2:T(8,128)(2,1)S(1)} %get-tuple-element.446), channel_id=1, source_target_pairs={{0,24},{4,28},{8,16},{12,20},{16,8},{20,12},{24,0},{28,4},{1,25},{... | collective-permute-start | bytes 49160 | tf_op jit(solution)/shard_map/ppermute | solution.py:18
  91.9 4.9 %collective-permute-start.6 = (bf16[1,16,4,128]{3,1,0,2:T(8,128)(2,1)S(1)}, bf16[1,16,4,128]{3,1,0,2:T(8,128)(2,1)S(1)}, u32[]{:S(2)}, u32[]{:S(2)}) collective-permute-start(bf16[1,16,4,128]{3,1,0,2:T(8,128)(2,1)S(1)} %get-tuple-element.445), channel_id=1, source_target_pairs={{0,28},{4,24},{8,20},{12,16},{16,12},{20,8},{24,4},{28,0},{1,29},{... | collective-permute-start | bytes 49160 | tf_op jit(solution)/shard_map/ppermute | solution.py:18
  132.5 0.8 copy-start.7
